TPU v7x, 256 devices: a whole 4x4x8 slice. The times are simulated.
256 devices in a mesh: dp: 32 (over x, y, core), mp: 8 (over z).
Axes of the slice: x: 4, y: 4, z: 8, core: 2. Of those that a mesh axis runs over, the one named last changes fastest.
Arguments:
- hidden: bfloat16 [512, 1024], P('dp'), may hold values from -6 to 6
- attn_gain: float32 [1024], replicated, may hold values from 0.25 to 1.75
- w_qkv: bfloat16 [1024, 3, 1024], P(None, None, 'mp'), may hold values from -2 to 2
- w_out: bfloat16 [1024, 1024], P('mp'), may hold values from -0.1875 to 0.1875
- mlp_gain: float32 [1024], replicated, may hold values from 0.25 to 1.75
- w_gate_up: bfloat16 [1024, 2, 4096], P(None, None, 'mp'), may hold values from -0.1875 to 0.1875
- w_down: bfloat16 [4096, 1024], P('mp'), may hold values from -0.09375 to 0.09375
- kv_cache: bfloat16 [2, 4096, 128, 1024], P(None, 'dp', None, 'mp'), may hold values from -9 to 9
- lengths: int32 [512], replicated, may hold values from 1 to 16384, as said below
- page_request: int32 [4096], P('dp'), may hold values from -1 to 511, as said below
- page_index: int32 [4096], P('dp'), may hold values from 0 to 127, as said below
Outputs:
- appended: bfloat16 [2, 512, 1024], P(None, 'dp', 'mp')
- hidden_out: bfloat16 [512, 1024], P('dp')
Inputs may be any that keep to these rules, and one draw needn't show every extreme that they name: `lengths`: 4 requests hold exactly 16384 tokens, the others fewer than 512. `page_request`: each request owns exactly ceil(lengths / 128) pool pages, which may lie on any data devices; -1 marks an empty page. `page_index`: the pages of a request carry the places 0 to ceil(lengths / 128) - 1, each once; empty pages carry 0.
All inputs are finite; a program needn't handle non-finite values.
Results may differ from a plain program's by a relative error of at most 0.0085.
Values may be sent and summed in bfloat16 or wider, within the bound.
No kernel may reach another device: no remote copies, remote signals or barrier semaphores. Data moves between devices by JAX's collectives and lax.ppermute only.
A program may use at most 128 MiB of HBM per device.

v0:
```python
import jax
import jax.numpy as jnp
from jax import lax
from jax.sharding import PartitionSpec as P

HEAD_DIM = 64
PAGE_BLOCK = 8
EPSILON = 1e-05
NEGATIVE = -1e30


def merged_2(value, axis, join):
    pieces = jax.tree.map(lambda part: lax.all_gather(part, axis), value)
    head = jax.tree.map(lambda part: part[0], pieces)
    tail = jax.tree.map(lambda part: part[1:], pieces)
    running, _ = lax.scan(lambda running, piece: (join(running, piece), None), head, tail)
    return running


def rms_norm(values, gain):
    widened = values.astype(jnp.float32)
    mean_square = jnp.mean(widened * widened, axis=-1, keepdims=True)
    return (widened * lax.rsqrt(mean_square + EPSILON) * gain).astype(jnp.bfloat16)


def combine(first, second):
    largest = jnp.maximum(first[0], second[0])
    shrink_first = jnp.exp(first[0] - largest)
    shrink_second = jnp.exp(second[0] - largest)
    totals = first[1] * shrink_first + second[1] * shrink_second
    weighted = first[2] * shrink_first[:, :, None] + second[2] * shrink_second[:, :, None]
    return (largest, totals, weighted)


def body(
    hidden,
    attn_gain,
    w_qkv,
    w_out,
    mlp_gain,
    w_gate_up,
    w_down,
    kv_cache,
    lengths,
    page_request,
    page_index,
):
    local_rows = hidden.shape[0]
    head_cols = w_qkv.shape[2]
    local_heads = head_cols // HEAD_DIM
    pool_pages = kv_cache.shape[1]
    page_len = kv_cache.shape[2]
    data_devices = lax.axis_size("dp")
    requests = local_rows * data_devices
    score_scale = HEAD_DIM ** (-0.5)
    normed = rms_norm(hidden, attn_gain)
    projected = jnp.dot(
        normed, w_qkv.reshape(w_qkv.shape[0], 3 * head_cols), preferred_element_type=jnp.float32
    )
    projected = lax.optimization_barrier(projected.astype(jnp.bfloat16)).reshape(
        local_rows, 3, head_cols
    )
    appended = jnp.stack([projected[:, 1], projected[:, 2]])
    every_query = lax.all_gather(projected[:, 0], "dp", axis=0, tiled=True)
    own_queries = projected[:, 0].reshape(local_rows, local_heads, HEAD_DIM).astype(jnp.float32)
    own_keys = projected[:, 1].reshape(local_rows, local_heads, HEAD_DIM).astype(jnp.float32)
    own_values = projected[:, 2].reshape(local_rows, local_heads, HEAD_DIM).astype(jnp.float32)
    self_scores = jnp.sum(own_queries * own_keys, axis=-1) * score_scale
    home_row = lax.axis_index("dp") * local_rows
    start_max = lax.dynamic_update_slice(
        jnp.full((requests, local_heads), NEGATIVE, jnp.float32), self_scores, (home_row, 0)
    )
    start_totals = lax.dynamic_update_slice(
        jnp.zeros((requests, local_heads), jnp.float32),
        jnp.ones((local_rows, local_heads), jnp.float32),
        (home_row, 0),
    )
    start_weighted = lax.dynamic_update_slice(
        jnp.zeros((requests, local_heads, HEAD_DIM), jnp.float32), own_values, (home_row, 0, 0)
    )
    visit_order = jnp.arange(pool_pages, dtype=jnp.int32)
    trip_count = pool_pages // PAGE_BLOCK
    request_ids = jnp.arange(requests, dtype=jnp.int32)
    offsets = jnp.arange(page_len, dtype=jnp.int32)

    def visit(step_index, carry):
        running_max, totals, weighted = carry
        picked = lax.dynamic_slice_in_dim(visit_order, step_index * PAGE_BLOCK, PAGE_BLOCK, 0)
        fetched = jnp.take(kv_cache, picked, axis=1)
        owners = page_request[picked]
        page_pos = page_index[picked]
        clamped = jnp.maximum(owners, 0)
        chosen_queries = every_query[clamped].reshape(PAGE_BLOCK, local_heads, HEAD_DIM)
        key_rows = fetched[0].reshape(PAGE_BLOCK, page_len, local_heads, HEAD_DIM)
        value_rows = fetched[1].reshape(PAGE_BLOCK, page_len, local_heads, HEAD_DIM)
        scores = (
            jnp.einsum(
                "phd,pthd->pht", chosen_queries, key_rows, preferred_element_type=jnp.float32
            )
            * score_scale
        )
        position = page_pos[:, None] * page_len + offsets[None, :]
        usable = (owners[:, None] >= 0) & (position < lengths[clamped][:, None])
        page_max = jnp.max(jnp.where(usable[:, None, :], scores, NEGATIVE), axis=2)
        raw = jnp.where(usable[:, None, :], jnp.exp(scores - page_max[:, :, None]), 0.0)
        page_total = jnp.sum(raw, axis=2)
        page_sum = jnp.einsum(
            "pht,pthd->phd",
            raw.astype(jnp.bfloat16),
            value_rows,
            preferred_element_type=jnp.float32,
        )
        member = owners[:, None] == request_ids[None, :]
        candidate = jnp.max(jnp.where(member[:, :, None], page_max[:, None, :], NEGATIVE), axis=0)
        new_max = jnp.maximum(running_max, candidate)
        factors = jnp.where(owners[:, None] >= 0, jnp.exp(page_max - new_max[clamped]), 0.0)
        rescale = jnp.exp(running_max - new_max)
        onehot = member.astype(jnp.float32)
        totals = totals * rescale + jnp.einsum(
            "pr,ph->rh", onehot, page_total * factors, precision=lax.Precision.HIGHEST
        )
        weighted = weighted * rescale[:, :, None] + jnp.einsum(
            "pr,phd->rhd", onehot, page_sum * factors[:, :, None], precision=lax.Precision.HIGHEST
        )
        return (new_max, totals, weighted)

    running_max, totals, weighted = lax.fori_loop(
        0, trip_count, visit, (start_max, start_totals, start_weighted)
    )
    merged = merged_2((running_max, totals, weighted), "dp", combine)
    own_totals = lax.dynamic_slice_in_dim(merged[1], home_row, local_rows, 0)
    own_weighted = lax.dynamic_slice_in_dim(merged[2], home_row, local_rows, 0)
    context = (
        (own_weighted / own_totals[:, :, None]).reshape(local_rows, head_cols).astype(jnp.bfloat16)
    )
    attended = lax.psum(jnp.dot(context, w_out, preferred_element_type=jnp.float32), "mp")
    residual = lax.optimization_barrier(
        (hidden.astype(jnp.float32) + attended).astype(jnp.bfloat16)
    )
    normed_mlp = rms_norm(residual, mlp_gain)
    hidden_cols = w_gate_up.shape[2]
    gate_up = jnp.dot(
        normed_mlp,
        w_gate_up.reshape(w_gate_up.shape[0], 2 * hidden_cols),
        preferred_element_type=jnp.float32,
    ).reshape(local_rows, 2, hidden_cols)
    activated = (jax.nn.silu(gate_up[:, 0]) * gate_up[:, 1]).astype(jnp.bfloat16)
    lowered = lax.psum(jnp.dot(activated, w_down, preferred_element_type=jnp.float32), "mp")
    hidden_out = (residual.astype(jnp.float32) + lowered).astype(jnp.bfloat16)
    return (appended, hidden_out)


def solution(mesh):
    return jax.shard_map(
        body,
        mesh=mesh,
        in_specs=(
            P("dp", None),
            P(),
            P(None, None, "mp"),
            P("mp", None),
            P(),
            P(None, None, "mp"),
            P("mp", None),
            P(None, "dp", None, "mp"),
            P(),
            P("dp"),
            P("dp"),
        ),
        out_specs=(P(None, "dp", "mp"), P("dp", None)),
        check_vma=False,
    )
```

profile of v0, /device:TPU:2, one launch (start us, length us, event | category | flops | bytes accessed | tf_op | source)
XLA Modules:
  0.0 589.8 jit_solution(4555764252407409945)
XLA Ops:
  11.2 24.7 %all-gather = bf16[512,1,128]{2,0,1:T(8,128)(2,1)S(1)} all-gather(bf16[16,1,128]{2,0,1:T(8,128)(2,1)S(1)} %copy.113), channel_id=2, replica_groups=mesh['dp'=32,'mp'=8] {'dp'}, dimensions={0}, use_global_device_ids=true | all-gather | bytes 135168 | tf_op jit(solution)/shard_map/all_gather | solution.py:64
  36.7 190.9 %while.35 = (s32[]{:T(128)}, f32[512,2]{0,1:T(2,128)S(1)}, f32[512,2]{0,1:T(2,128)S(1)}, f32[512,2,64]{0,2,1:T(8,128)S(1)}, s32[128]{0:T(128)S(1)}, /*index=5*/s...) while((s32[]{:T(128)}, f32[512,2]{0,1:T(2,128)S(1)}, ...), condition=%wide.region_6.7_spmd.clone.clone, body=%wide.region_2.6_spmd.clone.clone.sunk | while | flops 7361630 | bytes 5361311 | solution.py:127
  41.5 4.0 gather_fusion.2
  53.5 4.0 gather_fusion.2
  65.4 4.0 gather_fusion.2
  77.3 4.0 gather_fusion.2
  89.3 4.0 gather_fusion.2
  101.2 4.0 gather_fusion.2
  113.1 4.0 gather_fusion.2
  125.1 4.0 gather_fusion.2
  137.0 4.0 gather_fusion.2
  148.9 4.0 gather_fusion.2
  160.9 4.0 gather_fusion.2
  172.8 4.0 gather_fusion.2
  184.7 4.0 gather_fusion.2
  196.7 4.0 gather_fusion.2
  208.6 4.0 gather_fusion.2
  220.5 4.0 gather_fusion.2
  228.4 22.8 %all-gather.1 = f32[16384,2]{0,1:T(2,128)S(1)} all-gather(f32[512,2]{0,1:T(2,128)S(1)} %get-tuple-element.259), channel_id=3, replica_groups=mesh['dp'=32,'mp'=8] {'dp'}, dimensions={0}, use_global_device_ids=true | all-gather | bytes 135168 | tf_op jit(solution)/shard_map/all_gather | solution.py:13
  251.2 24.6 %all-gather.2 = f32[16384,2]{0,1:T(2,128)S(1)} all-gather(f32[512,2]{0,1:T(2,128)S(1)} %get-tuple-element.260), channel_id=4, replica_groups=mesh['dp'=32,'mp'=8] {'dp'}, dimensions={0}, use_global_device_ids=true | all-gather | bytes 135168 | tf_op jit(solution)/shard_map/all_gather | solution.py:13
  275.8 12.0 %all-gather.6.cloned.1.call-done = f32[16384,2,64]{0,2,1:T(8,128)} async-done(((f32[512,2,64]{0,2,1:T(8,128)}), f32[16384,2,64]{0,2,1:T(8,128)}) %all-gather.6.cloned.1.call-update) | async-done | bytes 8388624 | tf_op jit(solution)/shard_map/all_gather | solution.py:13
  289.0 7.1 %slice.95 = f32[15872,2,64]{0,2,1:T(8,128)} slice(f32[16384,2,64]{0,2,1:T(8,128)} %all-gather.6.cloned.1.call-done), slice={[512:16384], [0:2], [0:64]} | slice | bytes 16252928 | tf_op jit(solution)/shard_map/slice | solution.py:15
  296.1 19.6 %copy.125 = f32[15872,2,64]{2,1,0:T(2,128)} copy(f32[15872,2,64]{0,2,1:T(8,128)} %slice.95) | data formatting | bytes 16252928 | tf_op jit(solution)/shard_map/while | solution.py:16
  315.7 119.1 %while.34 = (s32[]{:T(128)}, f32[512,2]{0,1:T(2,128)S(1)}, f32[512,2]{0,1:T(2,128)S(1)}, f32[512,2,64]{2,1,0:T(2,128)S(1)}, f32[31,512,2]{1,2,0:T(2,128)S(1)}, /...) while((s32[]{:T(128)}, f32[512,2]{0,1:T(2,128)S(1)}, f32[512,2]{0,1:T(2,128)S(1)}, ...), condition=%wide.region_8.9_spmd, body=%wide.region_7.8_spmd.sunk | while | flops 202754 | bytes 843877 | solution.py:16
  316.0 3.5 fusion.67
  319.8 3.5 fusion.67
  323.7 3.5 fusion.67
  327.5 3.5 fusion.67
  331.4 3.5 fusion.67
  436.0 3.5 copy.128
  442.4 65.8 %all-reduce.3.cloned.1.call-done = f32[16,1024]{1,0:T(8,128)} async-done(((f32[16,1024]{1,0:T(8,128)}), f32[16,1024]{1,0:T(8,128)}) %all-reduce.3.cloned.1.call-update) | async-done | bytes 65552 | tf_op jit(solution)/shard_map/psum | solution.py:136
  511.4 70.4 %all-reduce.5.cloned.1.call-done = f32[16,1024]{1,0:T(8,128)} async-done(((f32[16,1024]{1,0:T(8,128)}), f32[16,1024]{1,0:T(8,128)}) %all-reduce.5.cloned.1.call-update) | async-done | bytes 65552 | tf_op jit(solution)/shard_map/psum | solution.py:148
  (672 shorter events, 240.6 us)
Async XLA Ops:
  7.2 502.7 %copy-start = (bf16[512,1024]{1,0:T(8,128)(2,1)S(1)}, bf16[512,1024]{1,0:T(8,128)(2,1)}, u32[]{:S(2)}) copy-start(bf16[512,1024]{1,0:T(8,128)(2,1)} %param.21) | copy-start | bytes 3145732
  7.2 280.6 %all-gather.6.cloned.1.call-start = ((), (), s32[]{:S(2)}) async-start(), calls=%async_computation.2 | async-start | bytes 8650752 | tf_op jit(solution)/shard_map/all_gather | solution.py:13
  227.6 0.7 copy-start.1
  228.3 279.9 %all-reduce.3.cloned.1.call-start = ((), (), s32[]{:S(2)}) async-start(), calls=%async_computation | async-start | bytes 131072 | tf_op jit(solution)/shard_map/psum | solution.py:136
  315.6 119.5 %copy-start.3 = (bf16[128,1024]{1,0:T(8,128)(2,1)S(1)}, bf16[128,1024]{1,0:T(8,128)(2,1)}, u32[]{:S(2)}) copy-start(bf16[128,1024]{1,0:T(8,128)(2,1)} %param.18) | copy-start | bytes 786436
  315.7 192.6 %copy-start.2 = (bf16[16,1024]{1,0:T(8,128)(2,1)S(1)}, bf16[16,1024]{1,0:T(8,128)(2,1)}, u32[]{:S(2)}) copy-start(bf16[16,1024]{1,0:T(8,128)(2,1)} %param.15) | copy-start | bytes 98308
  315.7 193.5 %copy-start.4 = (f32[1024]{0:T(1024)S(1)}, f32[1024]{0:T(1024)}, u32[]{:S(2)}) copy-start(f32[1024]{0:T(1024)} %param.19) | copy-start | bytes 12292
  436.0 145.8 %all-reduce.5.cloned.1.call-start = ((), (), s32[]{:S(2)}) async-start(), calls=%async_computation.1 | async-start | bytes 131072 | tf_op jit(solution)/shard_map/psum | solution.py:148
Sparse Core Ops, SparseCore 0:
  228.4 59.3 all-gather.5
  436.1 72.0 all-reduce.2
  510.9 70.8 all-reduce.4
where the time goes:
time: 593 us; the launch traced here: 590 us
  local copies, waits for them, and re-layouts  206 us (35%)
  waiting for transfers between devices  148 us (25%)
  other arithmetic  126 us (21%)
  blocking collectives  72.1 us (12%)
  matrix products  20.3 us (3%)
  between operations  13.9 us (2%)
    add x31, other arithmetic, combine(): first[2] * shrink_first[:, :, None] + second[2] * shrink_second[:, :, None]  108 us
    psum x1, waiting for transfers between devices, body(): lax.psum(jnp.dot(activated, w_down, preferred_element_type=jnp.float32),...  70.4 us
    psum x1, waiting for transfers between devices, body(): lax.psum(jnp.dot(context, w_out, preferred_element_type=jnp.float32), 'mp')  65.8 us
    gather x16, local copies, waits for them, and re-layouts, visit(): fetched = jnp.take(kv_cache, picked, axis=1)  64.4 us
    all_gather x2, blocking collectives, merged_2(): pieces = jax.tree.map(lambda part: lax.all_gather(part, axis), value)  47.4 us
    all_gather x1, blocking collectives, body(): every_query = lax.all_gather(projected[:, 0], 'dp', axis=0, tiled=True)  24.7 us
    gather x16, local copies, waits for them, and re-layouts, visit(): usable = (owners[:, None] >= 0) & (position < lengths[clamped][:, None])  21.2 us
    gather x16, local copies, waits for them, and re-layouts, visit(): owners = page_request[picked]  20.8 us
  transfers between devices with their start and end apart: 3, of which 3 were waited for; matrix products, arithmetic and copies ran while one was open for 1% of the time, Pallas kernels for 0%

commit v1 on v0

--- a/solution.py
+++ b/solution.py
@@ -61,7 +61,14 @@
         local_rows, 3, head_cols
     )
     appended = jnp.stack([projected[:, 1], projected[:, 2]])
-    every_query = lax.all_gather(projected[:, 0], "dp", axis=0, tiled=True)
+    sheet = projected[:, 0]
+    leaves = []
+    for _ in range(lax.axis_size("dp")):
+        leaves.append(sheet)
+    every_query = jnp.concatenate(
+        lax.all_to_all(jnp.stack(leaves, axis=0), axis_name="dp", split_axis=0, concat_axis=0),
+        axis=0,
+    )
     own_queries = projected[:, 0].reshape(local_rows, local_heads, HEAD_DIM).astype(jnp.float32)
     own_keys = projected[:, 1].reshape(local_rows, local_heads, HEAD_DIM).astype(jnp.float32)
     own_values = projected[:, 2].reshape(local_rows, local_heads, HEAD_DIM).astype(jnp.float32)

time: 593 us -> 581 us (0.980)
  blocking collectives: 72.1 us -> 46.2 us
  starting transfers between devices: 0.12 us -> 7.75 us
  waiting for transfers between devices: 148 us -> 154 us
    all_gather x1 -> x0, blocking collectives: 24.7 us -> none  [body(): every_query = lax.all_gather(projected[:, 0], 'dp', axis=0, tiled=True)]
    all_to_all x0 -> x1, starting transfers between devices: none -> 7.62 us  [body(): lax.all_to_all(jnp.stack(leaves, axis=0), axis_name='dp', split_axis=0, c...]
  transfers between devices with their start and end apart: 3 -> 4, of which waited for: 3 -> 4; matrix products, arithmetic and copies ran while one was open for 1% -> 1% of each run, Pallas kernels for 0% -> 0%
where the time goes in v1:
time: 581 us; the launch traced here: 578 us
  local copies, waits for them, and re-layouts  207 us (36%)
  waiting for transfers between devices  154 us (27%)
  other arithmetic  126 us (22%)
  blocking collectives  46.2 us (8%)
  matrix products  20.4 us (4%)
  between operations  14 us (2%)
  starting transfers between devices  7.75 us (1%)
    add x31, other arithmetic, combine(): first[2] * shrink_first[:, :, None] + second[2] * shrink_second[:, :, None]  108 us
    psum x1, waiting for transfers between devices, body(): lax.psum(jnp.dot(activated, w_down, preferred_element_type=jnp.float32),...  70.4 us
    psum x1, waiting for transfers between devices, body(): lax.psum(jnp.dot(context, w_out, preferred_element_type=jnp.float32), 'mp')  66 us
    gather x16, local copies, waits for them, and re-layouts, visit(): fetched = jnp.take(kv_cache, picked, axis=1)  64.4 us
    all_gather x2, blocking collectives, merged_2(): pieces = jax.tree.map(lambda part: lax.all_gather(part, axis), value)  46.2 us
    gather x16, local copies, waits for them, and re-layouts, visit(): usable = (owners[:, None] >= 0) & (position < lengths[clamped][:, None])  21.2 us
    gather x16, local copies, waits for them, and re-layouts, visit(): owners = page_request[picked]  20.8 us
    gather x16, local copies, waits for them, and re-layouts, visit(): page_pos = page_index[picked]  20.8 us
  transfers between devices with their start and end apart: 4, of which 4 were waited for; matrix products, arithmetic and copies ran while one was open for 1% of the time, Pallas kernels for 0%

profile of v1, /device:TPU:2, one launch (start us, length us, event | category | flops | bytes accessed | tf_op | source)
XLA Modules:
  0.0 577.6 jit_solution(1713984487491552709)
XLA Ops:
  11.4 7.6 %all-to-all-start = ((bf16[32,16,128]{2,1,0:T(8,128)(2,1)}), bf16[32,16,128]{2,1,0:T(8,128)(2,1)S(1)}, u32[]{:S(2)}, u32[]{:S(2)}) async-start(bf16[32,16,128]{2,1,0:T(8,128)(2,1)} %stack.7), calls=%async_computation | async-start | bytes 262144 | tf_op jit(solution)/shard_map/all_to_all | solution.py:69
  20.3 5.3 all-to-all-done
  25.6 190.9 %while.35 = (s32[]{:T(128)}, f32[512,2]{0,1:T(2,128)S(1)}, f32[512,2]{0,1:T(2,128)S(1)}, f32[512,2,64]{0,2,1:T(8,128)S(1)}, s32[128]{0:T(128)S(1)}, /*index=5*/s...) while((s32[]{:T(128)}, f32[512,2]{0,1:T(2,128)S(1)}, ...), condition=%wide.region_6.7_spmd.clone.clone, body=%wide.region_2.6_spmd.clone.clone.sunk | while | flops 7361630 | bytes 5361311 | solution.py:134
  30.5 4.0 gather_fusion.2
  42.4 4.0 gather_fusion.2
  54.3 4.0 gather_fusion.2
  66.3 4.0 gather_fusion.2
  78.2 4.0 gather_fusion.2
  90.1 4.0 gather_fusion.2
  102.1 4.0 gather_fusion.2
  114.0 4.0 gather_fusion.2
  126.0 4.0 gather_fusion.2
  137.9 4.0 gather_fusion.2
  149.8 4.0 gather_fusion.2
  161.8 4.0 gather_fusion.2
  173.7 4.0 gather_fusion.2
  185.6 4.0 gather_fusion.2
  197.6 4.0 gather_fusion.2
  209.5 4.0 gather_fusion.2
  217.3 23.1 %all-gather = f32[16384,2]{0,1:T(2,128)S(1)} all-gather(f32[512,2]{0,1:T(2,128)S(1)} %get-tuple-element.259), channel_id=2, replica_groups=mesh['dp'=32,'mp'=8] {'dp'}, dimensions={0}, use_global_device_ids=true | all-gather | bytes 135168 | tf_op jit(solution)/shard_map/all_gather | solution.py:13
  240.5 23.1 %all-gather.1 = f32[16384,2]{0,1:T(2,128)S(1)} all-gather(f32[512,2]{0,1:T(2,128)S(1)} %get-tuple-element.260), channel_id=3, replica_groups=mesh['dp'=32,'mp'=8] {'dp'}, dimensions={0}, use_global_device_ids=true | all-gather | bytes 135168 | tf_op jit(solution)/shard_map/all_gather | solution.py:13
  263.6 11.8 %all-gather.5.cloned.1.call-done = f32[16384,2,64]{0,2,1:T(8,128)} async-done(((f32[512,2,64]{0,2,1:T(8,128)}), f32[16384,2,64]{0,2,1:T(8,128)}) %all-gather.5.cloned.1.call-update) | async-done | bytes 8388624 | tf_op jit(solution)/shard_map/all_gather | solution.py:13
  276.7 7.1 %slice.95 = f32[15872,2,64]{0,2,1:T(8,128)} slice(f32[16384,2,64]{0,2,1:T(8,128)} %all-gather.5.cloned.1.call-done), slice={[512:16384], [0:2], [0:64]} | slice | bytes 16252928 | tf_op jit(solution)/shard_map/slice | solution.py:15
  283.7 19.6 %copy.122 = f32[15872,2,64]{2,1,0:T(2,128)} copy(f32[15872,2,64]{0,2,1:T(8,128)} %slice.95) | data formatting | bytes 16252928 | tf_op jit(solution)/shard_map/while | solution.py:16
  303.3 119.1 %while.34 = (s32[]{:T(128)}, f32[512,2]{0,1:T(2,128)S(1)}, f32[512,2]{0,1:T(2,128)S(1)}, f32[512,2,64]{2,1,0:T(2,128)S(1)}, f32[31,512,2]{1,2,0:T(2,128)S(1)}, /...) while((s32[]{:T(128)}, f32[512,2]{0,1:T(2,128)S(1)}, f32[512,2]{0,1:T(2,128)S(1)}, ...), condition=%wide.region_8.9_spmd, body=%wide.region_7.8_spmd.sunk | while | flops 202754 | bytes 843877 | solution.py:16
  303.6 3.5 fusion.67
  307.5 3.5 fusion.67
  311.3 3.5 fusion.67
  315.2 3.5 fusion.67
  423.7 3.5 copy.126
  430.0 66.0 %all-reduce.3.cloned.1.call-done = f32[16,1024]{1,0:T(8,128)} async-done(((f32[16,1024]{1,0:T(8,128)}), f32[16,1024]{1,0:T(8,128)}) %all-reduce.3.cloned.1.call-update) | async-done | bytes 65552 | tf_op jit(solution)/shard_map/psum | solution.py:143
  499.2 70.4 %all-reduce.5.cloned.1.call-done = f32[16,1024]{1,0:T(8,128)} async-done(((f32[16,1024]{1,0:T(8,128)}), f32[16,1024]{1,0:T(8,128)}) %all-reduce.5.cloned.1.call-update) | async-done | bytes 65552 | tf_op jit(solution)/shard_map/psum | solution.py:155
  (674 shorter events, 244.9 us)
Async XLA Ops:
  7.2 490.5 %copy-start = (bf16[512,1024]{1,0:T(8,128)(2,1)S(1)}, bf16[512,1024]{1,0:T(8,128)(2,1)}, u32[]{:S(2)}) copy-start(bf16[512,1024]{1,0:T(8,128)(2,1)} %param.21) | copy-start | bytes 3145732
  11.4 14.2 %all-to-all-start = ((bf16[32,16,128]{2,1,0:T(8,128)(2,1)}), bf16[32,16,128]{2,1,0:T(8,128)(2,1)S(1)}, u32[]{:S(2)}, u32[]{:S(2)}) async-start(bf16[32,16,128]{2,1,0:T(8,128)(2,1)} %stack.7), calls=%async_computation | async-start | bytes 262144 | tf_op jit(solution)/shard_map/all_to_all | solution.py:69
  19.0 256.4 %all-gather.5.cloned.1.call-start = ((), (), s32[]{:S(2)}) async-start(), calls=%async_computation.3 | async-start | bytes 8650752 | tf_op jit(solution)/shard_map/all_gather | solution.py:13
  216.6 0.7 copy-start.1
  217.3 278.7 %all-reduce.3.cloned.1.call-start = ((), (), s32[]{:S(2)}) async-start(), calls=%async_computation.1 | async-start | bytes 131072 | tf_op jit(solution)/shard_map/psum | solution.py:143
  303.3 119.5 %copy-start.3 = (bf16[128,1024]{1,0:T(8,128)(2,1)S(1)}, bf16[128,1024]{1,0:T(8,128)(2,1)}, u32[]{:S(2)}) copy-start(bf16[128,1024]{1,0:T(8,128)(2,1)} %param.18) | copy-start | bytes 786436
  303.3 192.7 %copy-start.2 = (bf16[16,1024]{1,0:T(8,128)(2,1)S(1)}, bf16[16,1024]{1,0:T(8,128)(2,1)}, u32[]{:S(2)}) copy-start(bf16[16,1024]{1,0:T(8,128)(2,1)} %param.15) | copy-start | bytes 98308
  303.3 193.7 %copy-start.4 = (f32[1024]{0:T(1024)S(1)}, f32[1024]{0:T(1024)}, u32[]{:S(2)}) copy-start(f32[1024]{0:T(1024)} %param.19) | copy-start | bytes 12292
  423.6 146.0 %all-reduce.5.cloned.1.call-start = ((), (), s32[]{:S(2)}) async-start(), calls=%async_computation.2 | async-start | bytes 131072 | tf_op jit(solution)/shard_map/psum | solution.py:155
Sparse Core Ops, SparseCore 0:
  217.4 57.9 all-gather.4
  423.7 72.2 all-reduce.2
  498.7 70.8 all-reduce.4
